TPU v7x, 512 devices: a whole 4x4x16 slice. The times are simulated.
512 devices in a mesh: ta: 32 (over x_hi, z), gz: 8 (over y, x_lo), gy: 2 (over core).
Axes of the slice: x: 4 (x_hi: 2, x_lo: 2; x = x_hi * 2 + x_lo), y: 4, z: 16, core: 2. Of those that a mesh axis runs over, the one named last changes fastest.
Arguments:
- source_field: bfloat16 [32, 16, 4, 2, 256, 128], P('ta', 'gz', 'gy'), may hold values from -6 to 6
- clover: bfloat16 [32, 16, 4, 2, 128, 128], P('ta', 'gz', 'gy'), may hold values from -0.1875 to 0.1875
- forward: bfloat16 [4, 32, 16, 4, 2, 128, 128], P(None, 'ta', 'gz', 'gy'), may hold values from -0.1875 to 0.1875
- backward: bfloat16 [4, 32, 16, 4, 2, 128, 128], P(None, 'ta', 'gz', 'gy'), may hold values from -0.1875 to 0.1875
- restrict_blocks: bfloat16 [32, 16, 4, 2, 128, 128], P('ta', 'gz', 'gy'), may hold values from -0.1875 to 0.1875
Outputs:
- second_image: bfloat16 [32, 16, 4, 2, 256, 128], P('ta', 'gz', 'gy')
- restricted: bfloat16 [32, 16, 256, 128], P('ta')
All inputs are finite; a program needn't handle non-finite values.
Results may differ from a plain program's by a relative error of at most 0.0064.
Values may be sent and summed in bfloat16 or wider, within the bound.
No kernel may reach another device: no remote copies, remote signals or barrier semaphores. Data moves between devices by JAX's collectives and lax.ppermute only.
A program may use at most 64 MiB of HBM per device.

v0:
```python
import jax
import jax.numpy as jnp
from jax import lax
from jax.sharding import PartitionSpec as P


def padded_2(block, sides, width):
    for axis, dim in sides:
        count = lax.axis_size(axis)
        forward = [(i, i + 1) for i in range(count - 1)]
        forward.append((count - 1, 0))
        backward = [(target, source) for source, target in forward]
        low = lax.ppermute(
            lax.slice_in_dim(block, block.shape[dim] - width, None, axis=dim), axis, forward
        )
        high = lax.ppermute(lax.slice_in_dim(block, 0, width, axis=dim), axis, backward)
        block = jnp.concatenate([low, block, high], axis=dim)
    return block


def shifted(block, axis, distance):
    devices = range(lax.axis_size(axis))
    route = [((i - distance) % len(devices), i) for i in devices]
    return lax.ppermute(block, axis, route)


def apply_block(blocks, vector):
    return jnp.einsum("tzyxij,tzyxrj->tzyxri", blocks, vector, preferred_element_type=jnp.float32)


def settle(formed):
    return lax.optimization_barrier(formed).astype(jnp.float32)


def operate_raw(vector, clover, forward, backward, shifted_blocks):
    padded = padded_2(vector, (("ta", 0), ("gz", 1), ("gy", 2)), 1)
    total = apply_block(clover, vector)
    total = total + apply_block(forward[0], padded[2:, 1:-1, 1:-1])
    total = total + apply_block(forward[1], padded[1:-1, 2:, 1:-1])
    total = total + apply_block(forward[2], padded[1:-1, 1:-1, 2:])
    total = total + apply_block(forward[3], jnp.roll(vector, -1, axis=3))
    total = total + settle(
        apply_block(shifted_blocks[0], padded[:-2, 1:-1, 1:-1]).astype(jnp.bfloat16)
    )
    total = total + settle(
        apply_block(shifted_blocks[1], padded[1:-1, :-2, 1:-1]).astype(jnp.bfloat16)
    )
    total = total + settle(
        apply_block(shifted_blocks[2], padded[1:-1, 1:-1, :-2]).astype(jnp.bfloat16)
    )
    formed_x = apply_block(backward[3], vector).astype(jnp.bfloat16)
    total = total + settle(jnp.roll(formed_x, 1, axis=3))
    return total.astype(jnp.bfloat16)


def per_device(source_field, clover, forward, backward, restrict_blocks):
    back_time = backward[0]
    back_zdir = backward[1]
    back_ydir = backward[2]
    shifted_time = jnp.concatenate([shifted(back_time, "ta", 1), back_time[:-1]], axis=0)
    shifted_zdir = jnp.concatenate([shifted(back_zdir[:, -1:], "gz", 1), back_zdir[:, :-1]], axis=1)
    shifted_ydir = jnp.concatenate(
        [shifted(back_ydir[:, :, -1:], "gy", 1), back_ydir[:, :, :-1]], axis=2
    )
    shifted_blocks = (shifted_time, shifted_zdir, shifted_ydir)
    first_image = operate_raw(source_field, clover, forward, backward, shifted_blocks)
    second_image = operate_raw(first_image, clover, forward, backward, shifted_blocks)
    partial_sum = jnp.einsum(
        "tzyxij,tzyxrj->ri", restrict_blocks, second_image, preferred_element_type=jnp.float32
    )
    own_part = partial_sum.astype(jnp.bfloat16).reshape(
        1, 1, partial_sum.shape[0], partial_sum.shape[1]
    )
    restricted = lax.all_gather(own_part, ("gz", "gy"), axis=1, tiled=True)
    return (second_image, restricted)


def solution(mesh):
    return jax.shard_map(
        per_device,
        mesh=mesh,
        in_specs=(
            P("ta", "gz", "gy", None, None, None),
            P("ta", "gz", "gy", None, None, None),
            P(None, "ta", "gz", "gy", None, None, None),
            P(None, "ta", "gz", "gy", None, None, None),
            P("ta", "gz", "gy", None, None, None),
        ),
        out_specs=(P("ta", "gz", "gy", None, None, None), P("ta", None, None, None)),
        check_vma=False,
    )
```

profile of v0, /device:TPU:1, one launch (start us, length us, event | category | flops | bytes accessed | tf_op | source)
XLA Modules:
  0.0 204.1 jit_solution(7602025396160097925)
XLA Ops:
  7.2 4.5 %collective-permute-start.1 = (bf16[1,2,2,2,256,128]{5,4,3,2,1,0:T(8,128)(2,1)}, bf16[1,2,2,2,256,128]{5,4,3,2,1,0:T(8,128)(2,1)S(1)}, u32[]{:S(2)}, u32[]{:S(2)}) collective-permute-start(bf16[1,2,2,2,256,128]{5,4,3,2,1,0:T(8,128)(2,1)} %param.5), channel_id=1, source_target_pairs={{0,16},{16,32},{32,48},{48,64},{64,80},{80,96},{96,112},{112,128},... | collective-permute-start | bytes 1572872 | tf_op jit(solution)/shard_map/ppermute | solution.py:13
  11.7 12.0 %collective-permute-start = (bf16[1,2,2,2,256,128]{5,4,3,2,1,0:T(8,128)(2,1)}, bf16[1,2,2,2,256,128]{5,4,3,2,1,0:T(8,128)(2,1)S(1)}, u32[]{:S(2)}, u32[]{:S(2)}) collective-permute-start(bf16[1,2,2,2,256,128]{5,4,3,2,1,0:T(8,128)(2,1)} %param.5), channel_id=1, source_target_pairs={{16,0},{32,16},{48,32},{64,48},{80,64},{96,80},{112,96},{128,112},... | collective-permute-start | bytes 1572872 | tf_op jit(solution)/shard_map/ppermute | solution.py:16
  23.7 9.9 %collective-permute-done.1 = bf16[1,2,2,2,256,128]{5,4,3,2,1,0:T(8,128)(2,1)S(1)} collective-permute-done((bf16[1,2,2,2,256,128]{5,4,3,2,1,0:T(8,128)(2,1)}, bf16[1,2,2,2,256,128]{5,4,3,2,1,0:T(8,128)(2,1)S(1)}, u32[]{:S(2)}, u32[]{:S(2)}) %collective-permute-start.1) | collective-permute-done | bytes 524320 | tf_op jit(solution)/shard_map/ppermute | solution.py:13
  33.6 1.1 constant_dynamic-update-slice_fusion.1
  35.0 4.8 %collective-permute-start.2 = (bf16[3,1,2,2,256,128]{5,4,3,2,1,0:T(8,128)(2,1)S(1)}, bf16[3,1,2,2,256,128]{5,4,3,2,1,0:T(8,128)(2,1)S(1)}, u32[]{:S(2)}, u32[]{:S(2)}) collective-permute-start(bf16[3,1,2,2,256,128]{5,4,3,2,1,0:T(8,128)(2,1)S(1)} %get-tuple-element.9), channel_id=1, source_target_pairs={{2,0},{4,2},{6,4},{8,6},{10,8},{12,10},{14,12},{0,14},{3,1},{5,3},... | collective-permute-start | bytes 2359304 | tf_op jit(solution)/shard_map/ppermute | solution.py:16
  39.8 1.9 collective-permute-start.3
  41.9 3.6 %collective-permute-start.8 = (bf16[1,2,1,2,128,128]{5,4,3,2,1,0:T(8,128)(2,1)S(1)}, bf16[1,2,1,2,128,128]{5,4,3,2,1,0:T(8,128)(2,1)S(1)}, u32[]{:S(2)}, u32[]{:S(2)}) collective-permute-start(bf16[1,2,1,2,128,128]{5,4,3,2,1,0:T(8,128)(2,1)S(1)} %get-tuple-element.23), channel_id=1, source_target_pairs={{1,0},{0,1},{3,2},{2,3},{5,4},{4,5},{7,6},{6,7},{9,8},{8,9},{11,10... | collective-permute-start | bytes 393224 | tf_op jit(solution)/shard_map/ppermute | solution.py:24
  45.5 2.1 %collective-permute-start.6 = (bf16[1,1,2,2,128,128]{5,4,3,2,1,0:T(8,128)(2,1)S(1)}, bf16[1,1,2,2,128,128]{5,4,3,2,1,0:T(8,128)(2,1)S(1)}, u32[]{:S(2)}, u32[]{:S(2)}) collective-permute-start(bf16[1,1,2,2,128,128]{5,4,3,2,1,0:T(8,128)(2,1)S(1)} %get-tuple-element.21), channel_id=1, source_target_pairs={{14,0},{0,2},{2,4},{4,6},{6,8},{8,10},{10,12},{12,14},{15,1},{1,3}... | collective-permute-start | bytes 393224 | tf_op jit(solution)/shard_map/ppermute | solution.py:24
  47.6 1.9 collective-permute-start.5
  49.8 11.2 %collective-permute-done.2 = bf16[3,1,2,2,256,128]{5,4,3,2,1,0:T(8,128)(2,1)S(1)} collective-permute-done((bf16[3,1,2,2,256,128]{5,4,3,2,1,0:T(8,128)(2,1)S(1)}, bf16[3,1,2,2,256,128]{5,4,3,2,1,0:T(8,128)(2,1)S(1)}, u32[]{:S(2)}, u32[]{:S(2)}) %collective-permute-start.2) | collective-permute-done | bytes 786464 | tf_op jit(solution)/shard_map/ppermute | solution.py:16
  61.0 18.7 %collective-permute-done.3 = bf16[3,1,2,2,256,128]{5,4,3,2,1,0:T(8,128)(2,1)S(1)} collective-permute-done((bf16[3,1,2,2,256,128]{5,4,3,2,1,0:T(8,128)(2,1)S(1)}, bf16[3,1,2,2,256,128]{5,4,3,2,1,0:T(8,128)(2,1)S(1)}, u32[]{:S(2)}, u32[]{:S(2)}) %collective-permute-start.3) | collective-permute-done | bytes 786464 | tf_op jit(solution)/shard_map/ppermute | solution.py:13
  79.7 0.4 pad_maximum_fusion
  80.3 5.5 %collective-permute-start.7 = (bf16[3,4,1,2,256,128]{5,4,3,2,1,0:T(8,128)(2,1)S(1)}, bf16[3,4,1,2,256,128]{5,4,3,2,1,0:T(8,128)(2,1)S(1)}, u32[]{:S(2)}, u32[]{:S(2)}) collective-permute-start(bf16[3,4,1,2,256,128]{5,4,3,2,1,0:T(8,128)(2,1)S(1)} %get-tuple-element.4), channel_id=1, source_target_pairs={{0,1},{1,0},{2,3},{3,2},{4,5},{5,4},{6,7},{7,6},{8,9},{9,8},{10,11... | collective-permute-start | bytes 4718600 | tf_op jit(solution)/shard_map/ppermute | solution.py:13
  85.9 2.1 %collective-permute-start.4 = (bf16[3,4,1,2,256,128]{5,4,3,2,1,0:T(8,128)(2,1)S(1)}, bf16[3,4,1,2,256,128]{5,4,3,2,1,0:T(8,128)(2,1)S(1)}, u32[]{:S(2)}, u32[]{:S(2)}) collective-permute-start(bf16[3,4,1,2,256,128]{5,4,3,2,1,0:T(8,128)(2,1)S(1)} %get-tuple-element.5), channel_id=1, source_target_pairs={{1,0},{0,1},{3,2},{2,3},{5,4},{4,5},{7,6},{6,7},{9,8},{8,9},{11,10... | collective-permute-start | bytes 4718600 | tf_op jit(solution)/shard_map/ppermute | solution.py:16
  90.0 1.3 collective-permute-done.4
  91.6 0.6 fusion.15
  92.3 1.9 collective-permute-start.10
  94.2 7.0 %collective-permute-start.9 = (bf16[1,2,2,2,256,128]{5,4,3,2,1,0:T(8,128)(2,1)S(1)}, bf16[1,2,2,2,256,128]{5,4,3,2,1,0:T(8,128)(2,1)S(1)}, u32[]{:S(2)}, u32[]{:S(2)}) collective-permute-start(bf16[1,2,2,2,256,128]{5,4,3,2,1,0:T(8,128)(2,1)S(1)} %fusion.15), channel_id=1, source_target_pairs={{16,0},{32,16},{48,32},{64,48},{80,64},{96,80},{112,96},{128,112},... | collective-permute-start | bytes 1572872 | tf_op jit(solution)/shard_map/ppermute | solution.py:16
  101.2 9.9 %collective-permute-done.10 = bf16[1,2,2,2,256,128]{5,4,3,2,1,0:T(8,128)(2,1)S(1)} collective-permute-done((bf16[1,2,2,2,256,128]{5,4,3,2,1,0:T(8,128)(2,1)S(1)}, bf16[1,2,2,2,256,128]{5,4,3,2,1,0:T(8,128)(2,1)S(1)}, u32[]{:S(2)}, u32[]{:S(2)}) %collective-permute-start.10) | collective-permute-done | bytes 524320 | tf_op jit(solution)/shard_map/ppermute | solution.py:13
  111.1 0.9 collective-permute-done.9
  112.3 2.2 %collective-permute-start.12 = (bf16[3,1,2,2,256,128]{5,4,3,2,1,0:T(8,128)(2,1)S(1)}, bf16[3,1,2,2,256,128]{5,4,3,2,1,0:T(8,128)(2,1)S(1)}, u32[]{:S(2)}, u32[]{:S(2)}) collective-permute-start(bf16[3,1,2,2,256,128]{5,4,3,2,1,0:T(8,128)(2,1)S(1)} %get-tuple-element.6), channel_id=1, source_target_pairs={{0,2},{2,4},{4,6},{6,8},{8,10},{10,12},{12,14},{14,0},{1,3},{3,5},... | collective-permute-start | bytes 2359304 | tf_op jit(solution)/shard_map/ppermute | solution.py:13
  114.5 5.2 %collective-permute-start.11 = (bf16[3,1,2,2,256,128]{5,4,3,2,1,0:T(8,128)(2,1)S(1)}, bf16[3,1,2,2,256,128]{5,4,3,2,1,0:T(8,128)(2,1)S(1)}, u32[]{:S(2)}, u32[]{:S(2)}) collective-permute-start(bf16[3,1,2,2,256,128]{5,4,3,2,1,0:T(8,128)(2,1)S(1)} %get-tuple-element.7), channel_id=1, source_target_pairs={{2,0},{4,2},{6,4},{8,6},{10,8},{12,10},{14,12},{0,14},{3,1},{5,3},... | collective-permute-start | bytes 2359304 | tf_op jit(solution)/shard_map/ppermute | solution.py:16
  120.0 14.1 %collective-permute-done.12 = bf16[3,1,2,2,256,128]{5,4,3,2,1,0:T(8,128)(2,1)S(1)} collective-permute-done((bf16[3,1,2,2,256,128]{5,4,3,2,1,0:T(8,128)(2,1)S(1)}, bf16[3,1,2,2,256,128]{5,4,3,2,1,0:T(8,128)(2,1)S(1)}, u32[]{:S(2)}, u32[]{:S(2)}) %collective-permute-start.12) | collective-permute-done | bytes 786464 | tf_op jit(solution)/shard_map/ppermute | solution.py:13
  134.1 13.9 %collective-permute-done.11 = bf16[3,1,2,2,256,128]{5,4,3,2,1,0:T(8,128)(2,1)S(1)} collective-permute-done((bf16[3,1,2,2,256,128]{5,4,3,2,1,0:T(8,128)(2,1)S(1)}, bf16[3,1,2,2,256,128]{5,4,3,2,1,0:T(8,128)(2,1)S(1)}, u32[]{:S(2)}, u32[]{:S(2)}) %collective-permute-start.11) | collective-permute-done | bytes 786464 | tf_op jit(solution)/shard_map/ppermute | solution.py:16
  148.0 0.4 pad_maximum_fusion.1
  148.6 3.8 %collective-permute-start.14 = (bf16[3,4,1,2,256,128]{5,4,3,2,1,0:T(8,128)(2,1)S(1)}, bf16[3,4,1,2,256,128]{5,4,3,2,1,0:T(8,128)(2,1)S(1)}, u32[]{:S(2)}, u32[]{:S(2)}) collective-permute-start(bf16[3,4,1,2,256,128]{5,4,3,2,1,0:T(8,128)(2,1)S(1)} %get-tuple-element.2), channel_id=1, source_target_pairs={{0,1},{1,0},{2,3},{3,2},{4,5},{5,4},{6,7},{7,6},{8,9},{9,8},{10,11... | collective-permute-start | bytes 4718600 | tf_op jit(solution)/shard_map/ppermute | solution.py:13
  152.4 1.9 collective-permute-start.13
  156.4 1.4 collective-permute-done.13
  158.1 0.7 fusion.14
  159.0 0.9 fusion.24
  160.0 34.9 %all-gather.3.cloned.1.call-done = bf16[4096,128]{1,0:T(8,128)(2,1)} async-done(((bf16[256,128]{1,0:T(8,128)(2,1)}), bf16[4096,128]{1,0:T(8,128)(2,1)}) %all-gather.3.cloned.1.call-update) | async-done | bytes 1048592 | tf_op jit(solution)/shard_map/all_gather | solution.py:74
  194.9 2.3 %copy.17 = bf16[1,16,256,128]{3,2,1,0:T(8,128)(2,1)} copy(bf16[1,16,256,128]{3,2,1,0:T(8,128)(2,1)} %bitcast.156) | data formatting | bytes 2097152
  (52 shorter events, 6.6 us)
Async XLA Ops:
  7.2 81.2 %copy-start = (bf16[1,2,2,2,128,128]{5,4,3,2,1,0:T(8,128)(2,1)S(1)}, bf16[1,2,2,2,128,128]{5,4,3,2,1,0:T(8,128)(2,1)}, u32[]{:S(2)}) copy-start(bf16[1,2,2,2,128,128]{5,4,3,2,1,0:T(8,128)(2,1)} %param.6) | copy-start | bytes 786436
  7.2 187.7 %all-gather.3.cloned.1.call-start = ((), (), s32[]{:S(2)}) async-start(), calls=%async_computation | async-start | bytes 1114112 | tf_op jit(solution)/shard_map/all_gather | solution.py:74
  7.2 26.4 %collective-permute-start.1 = (bf16[1,2,2,2,256,128]{5,4,3,2,1,0:T(8,128)(2,1)}, bf16[1,2,2,2,256,128]{5,4,3,2,1,0:T(8,128)(2,1)S(1)}, u32[]{:S(2)}, u32[]{:S(2)}) collective-permute-start(bf16[1,2,2,2,256,128]{5,4,3,2,1,0:T(8,128)(2,1)} %param.5), channel_id=1, source_target_pairs={{0,16},{16,32},{32,48},{48,64},{64,80},{80,96},{96,112},{112,128},... | collective-permute-start | bytes 1572872 | tf_op jit(solution)/shard_map/ppermute | solution.py:13
  11.7 23.0 %collective-permute-start = (bf16[1,2,2,2,256,128]{5,4,3,2,1,0:T(8,128)(2,1)}, bf16[1,2,2,2,256,128]{5,4,3,2,1,0:T(8,128)(2,1)S(1)}, u32[]{:S(2)}, u32[]{:S(2)}) collective-permute-start(bf16[1,2,2,2,256,128]{5,4,3,2,1,0:T(8,128)(2,1)} %param.5), channel_id=1, source_target_pairs={{16,0},{32,16},{48,32},{64,48},{80,64},{96,80},{112,96},{128,112},... | collective-permute-start | bytes 1572872 | tf_op jit(solution)/shard_map/ppermute | solution.py:16
  34.8 6.9 %copy-start.3 = (bf16[4,1,2,2,2,128,128]{6,5,4,3,2,1,0:T(8,128)(2,1)S(1)}, bf16[4,1,2,2,2,128,128]{6,5,4,3,2,1,0:T(8,128)(2,1)}, u32[]{:S(2)}) copy-start(bf16[4,1,2,2,2,128,128]{6,5,4,3,2,1,0:T(8,128)(2,1)} %param.8) | copy-start | bytes 3145732
  35.0 14.5 %copy-start.1 = (bf16[1,2,2,2,256,128]{5,4,3,2,1,0:T(8,128)(2,1)S(1)}, bf16[1,2,2,2,256,128]{5,4,3,2,1,0:T(8,128)(2,1)}, u32[]{:S(2)}) copy-start(bf16[1,2,2,2,256,128]{5,4,3,2,1,0:T(8,128)(2,1)} %param.5) | copy-start | bytes 1572868
  35.0 25.9 %collective-permute-start.2 = (bf16[3,1,2,2,256,128]{5,4,3,2,1,0:T(8,128)(2,1)S(1)}, bf16[3,1,2,2,256,128]{5,4,3,2,1,0:T(8,128)(2,1)S(1)}, u32[]{:S(2)}, u32[]{:S(2)}) collective-permute-start(bf16[3,1,2,2,256,128]{5,4,3,2,1,0:T(8,128)(2,1)S(1)} %get-tuple-element.9), channel_id=1, source_target_pairs={{2,0},{4,2},{6,4},{8,6},{10,8},{12,10},{14,12},{0,14},{3,1},{5,3},... | collective-permute-start | bytes 2359304 | tf_op jit(solution)/shard_map/ppermute | solution.py:16
  39.8 39.9 %collective-permute-start.3 = (bf16[3,1,2,2,256,128]{5,4,3,2,1,0:T(8,128)(2,1)S(1)}, bf16[3,1,2,2,256,128]{5,4,3,2,1,0:T(8,128)(2,1)S(1)}, u32[]{:S(2)}, u32[]{:S(2)}) collective-permute-start(bf16[3,1,2,2,256,128]{5,4,3,2,1,0:T(8,128)(2,1)S(1)} %get-tuple-element.8), channel_id=1, source_target_pairs={{0,2},{2,4},{4,6},{6,8},{8,10},{10,12},{12,14},{14,0},{1,3},{3,5},... | collective-permute-start | bytes 2359304 | tf_op jit(solution)/shard_map/ppermute | solution.py:13
  41.9 47.8 %collective-permute-start.8 = (bf16[1,2,1,2,128,128]{5,4,3,2,1,0:T(8,128)(2,1)S(1)}, bf16[1,2,1,2,128,128]{5,4,3,2,1,0:T(8,128)(2,1)S(1)}, u32[]{:S(2)}, u32[]{:S(2)}) collective-permute-start(bf16[1,2,1,2,128,128]{5,4,3,2,1,0:T(8,128)(2,1)S(1)} %get-tuple-element.23), channel_id=1, source_target_pairs={{1,0},{0,1},{3,2},{2,3},{5,4},{4,5},{7,6},{6,7},{9,8},{8,9},{11,10... | collective-permute-start | bytes 393224 | tf_op jit(solution)/shard_map/ppermute | solution.py:24
  45.5 43.9 %collective-permute-start.6 = (bf16[1,1,2,2,128,128]{5,4,3,2,1,0:T(8,128)(2,1)S(1)}, bf16[1,1,2,2,128,128]{5,4,3,2,1,0:T(8,128)(2,1)S(1)}, u32[]{:S(2)}, u32[]{:S(2)}) collective-permute-start(bf16[1,1,2,2,128,128]{5,4,3,2,1,0:T(8,128)(2,1)S(1)} %get-tuple-element.21), channel_id=1, source_target_pairs={{14,0},{0,2},{2,4},{4,6},{6,8},{8,10},{10,12},{12,14},{15,1},{1,3}... | collective-permute-start | bytes 393224 | tf_op jit(solution)/shard_map/ppermute | solution.py:24
  47.6 41.5 %collective-permute-start.5 = (bf16[1,2,2,2,128,128]{5,4,3,2,1,0:T(8,128)(2,1)S(1)}, bf16[1,2,2,2,128,128]{5,4,3,2,1,0:T(8,128)(2,1)S(1)}, u32[]{:S(2)}, u32[]{:S(2)}) collective-permute-start(bf16[1,2,2,2,128,128]{5,4,3,2,1,0:T(8,128)(2,1)S(1)} %get-tuple-element.10), channel_id=1, source_target_pairs={{496,0},{0,16},{16,32},{32,48},{48,64},{64,80},{80,96},{96,112},{1... | collective-permute-start | bytes 786440 | tf_op jit(solution)/shard_map/ppermute | solution.py:24
  80.3 9.3 %collective-permute-start.7 = (bf16[3,4,1,2,256,128]{5,4,3,2,1,0:T(8,128)(2,1)S(1)}, bf16[3,4,1,2,256,128]{5,4,3,2,1,0:T(8,128)(2,1)S(1)}, u32[]{:S(2)}, u32[]{:S(2)}) collective-permute-start(bf16[3,4,1,2,256,128]{5,4,3,2,1,0:T(8,128)(2,1)S(1)} %get-tuple-element.4), channel_id=1, source_target_pairs={{0,1},{1,0},{2,3},{3,2},{4,5},{5,4},{6,7},{7,6},{8,9},{9,8},{10,11... | collective-permute-start | bytes 4718600 | tf_op jit(solution)/shard_map/ppermute | solution.py:13
  85.9 2.2 %copy-start.2 = (bf16[4,1,2,2,2,128,128]{6,5,4,3,2,1,0:T(8,128)(2,1)S(1)}, bf16[4,1,2,2,2,128,128]{6,5,4,3,2,1,0:T(8,128)(2,1)}, u32[]{:S(2)}) copy-start(bf16[4,1,2,2,2,128,128]{6,5,4,3,2,1,0:T(8,128)(2,1)} %param.7) | copy-start | bytes 3145732
  85.9 5.4 %collective-permute-start.4 = (bf16[3,4,1,2,256,128]{5,4,3,2,1,0:T(8,128)(2,1)S(1)}, bf16[3,4,1,2,256,128]{5,4,3,2,1,0:T(8,128)(2,1)S(1)}, u32[]{:S(2)}, u32[]{:S(2)}) collective-permute-start(bf16[3,4,1,2,256,128]{5,4,3,2,1,0:T(8,128)(2,1)S(1)} %get-tuple-element.5), channel_id=1, source_target_pairs={{1,0},{0,1},{3,2},{2,3},{5,4},{4,5},{7,6},{6,7},{9,8},{8,9},{11,10... | collective-permute-start | bytes 4718600 | tf_op jit(solution)/shard_map/ppermute | solution.py:16
  92.3 18.8 %collective-permute-start.10 = (bf16[1,2,2,2,256,128]{5,4,3,2,1,0:T(8,128)(2,1)S(1)}, bf16[1,2,2,2,256,128]{5,4,3,2,1,0:T(8,128)(2,1)S(1)}, u32[]{:S(2)}, u32[]{:S(2)}) collective-permute-start(bf16[1,2,2,2,256,128]{5,4,3,2,1,0:T(8,128)(2,1)S(1)} %fusion.15), channel_id=1, source_target_pairs={{0,16},{16,32},{32,48},{48,64},{64,80},{80,96},{96,112},{112,128},... | collective-permute-start | bytes 1572872 | tf_op jit(solution)/shard_map/ppermute | solution.py:13
  94.2 17.8 %collective-permute-start.9 = (bf16[1,2,2,2,256,128]{5,4,3,2,1,0:T(8,128)(2,1)S(1)}, bf16[1,2,2,2,256,128]{5,4,3,2,1,0:T(8,128)(2,1)S(1)}, u32[]{:S(2)}, u32[]{:S(2)}) collective-permute-start(bf16[1,2,2,2,256,128]{5,4,3,2,1,0:T(8,128)(2,1)S(1)} %fusion.15), channel_id=1, source_target_pairs={{16,0},{32,16},{48,32},{64,48},{80,64},{96,80},{112,96},{128,112},... | collective-permute-start | bytes 1572872 | tf_op jit(solution)/shard_map/ppermute | solution.py:16
  112.3 21.8 %collective-permute-start.12 = (bf16[3,1,2,2,256,128]{5,4,3,2,1,0:T(8,128)(2,1)S(1)}, bf16[3,1,2,2,256,128]{5,4,3,2,1,0:T(8,128)(2,1)S(1)}, u32[]{:S(2)}, u32[]{:S(2)}) collective-permute-start(bf16[3,1,2,2,256,128]{5,4,3,2,1,0:T(8,128)(2,1)S(1)} %get-tuple-element.6), channel_id=1, source_target_pairs={{0,2},{2,4},{4,6},{6,8},{8,10},{10,12},{12,14},{14,0},{1,3},{3,5},... | collective-permute-start | bytes 2359304 | tf_op jit(solution)/shard_map/ppermute | solution.py:13
  114.5 33.4 %collective-permute-start.11 = (bf16[3,1,2,2,256,128]{5,4,3,2,1,0:T(8,128)(2,1)S(1)}, bf16[3,1,2,2,256,128]{5,4,3,2,1,0:T(8,128)(2,1)S(1)}, u32[]{:S(2)}, u32[]{:S(2)}) collective-permute-start(bf16[3,1,2,2,256,128]{5,4,3,2,1,0:T(8,128)(2,1)S(1)} %get-tuple-element.7), channel_id=1, source_target_pairs={{2,0},{4,2},{6,4},{8,6},{10,8},{12,10},{14,12},{0,14},{3,1},{5,3},... | collective-permute-start | bytes 2359304 | tf_op jit(solution)/shard_map/ppermute | solution.py:16
  148.6 7.4 %collective-permute-start.14 = (bf16[3,4,1,2,256,128]{5,4,3,2,1,0:T(8,128)(2,1)S(1)}, bf16[3,4,1,2,256,128]{5,4,3,2,1,0:T(8,128)(2,1)S(1)}, u32[]{:S(2)}, u32[]{:S(2)}) collective-permute-start(bf16[3,4,1,2,256,128]{5,4,3,2,1,0:T(8,128)(2,1)S(1)} %get-tuple-element.2), channel_id=1, source_target_pairs={{0,1},{1,0},{2,3},{3,2},{4,5},{5,4},{6,7},{7,6},{8,9},{9,8},{10,11... | collective-permute-start | bytes 4718600 | tf_op jit(solution)/shard_map/ppermute | solution.py:13
  152.4 5.3 %collective-permute-start.13 = (bf16[3,4,1,2,256,128]{5,4,3,2,1,0:T(8,128)(2,1)S(1)}, bf16[3,4,1,2,256,128]{5,4,3,2,1,0:T(8,128)(2,1)S(1)}, u32[]{:S(2)}, u32[]{:S(2)}) collective-permute-start(bf16[3,4,1,2,256,128]{5,4,3,2,1,0:T(8,128)(2,1)S(1)} %get-tuple-element.3), channel_id=1, source_target_pairs={{1,0},{0,1},{3,2},{2,3},{5,4},{4,5},{7,6},{6,7},{9,8},{8,9},{11,10... | collective-permute-start | bytes 4718600 | tf_op jit(solution)/shard_map/ppermute | solution.py:16
  158.1 1.0 copy-start.5
  159.0 38.2 %copy-start.4 = (bf16[1,2,2,2,256,128]{5,4,3,2,1,0:T(8,128)(2,1)}, bf16[1,2,2,2,256,128]{5,4,3,2,1,0:T(8,128)(2,1)S(1)}, u32[]{:S(2)}) copy-start(bf16[1,2,2,2,256,128]{5,4,3,2,1,0:T(8,128)(2,1)S(1)} %fusion.14) | copy-start | bytes 1572868
Sparse Core Ops, SparseCore 0:
  160.1 34.7 all-gather.2
where the time goes:
time: 205 us; the launch traced here: 204 us
  waiting for transfers between devices  116 us (57%)
  starting transfers between devices  60.4 us (29%)
  between operations  14.5 us (7%)
  matrix products  7.1 us (3%)
  local copies, waits for them, and re-layouts  4.79 us (2%)
    ppermute x6, waiting for transfers between devices, padded_2(): lax.ppermute(lax.slice_in_dim(block, block.shape[dim] - width, None, axis...  52.6 us
    all_gather x1, waiting for transfers between devices, per_device(): restricted = lax.all_gather(own_part, ('gz', 'gy'), axis=1, tiled=True)  34.9 us
    ppermute x6, starting transfers between devices, padded_2(): lax.ppermute(lax.slice_in_dim(block, 0, width, axis=dim), axis, backward)  32.9 us
    ppermute x6, waiting for transfers between devices, padded_2(): lax.ppermute(lax.slice_in_dim(block, 0, width, axis=dim), axis, backward)  28.6 us
    ppermute x6, starting transfers between devices, padded_2(): lax.ppermute(lax.slice_in_dim(block, block.shape[dim] - width, None, axis...  19.9 us
    ppermute x3, starting transfers between devices, shifted(): return lax.ppermute(block, axis, route)  7.56 us
    dot_general x18, matrix products, apply_block(): jnp.einsum('tzyxij,tzyxrj->tzyxri', blocks, vector, preferred_element_typ...  6.17 us
  transfers between devices with their start and end apart: 16, of which 10 were waited for; matrix products, arithmetic and copies ran while one was open for 3% of the time, Pallas kernels for 0%

commit v1 on v0

--- a/solution.py
+++ b/solution.py
@@ -71,7 +71,10 @@
     own_part = partial_sum.astype(jnp.bfloat16).reshape(
         1, 1, partial_sum.shape[0], partial_sum.shape[1]
     )
-    restricted = lax.all_gather(own_part, ("gz", "gy"), axis=1, tiled=True)
+    restricted = jnp.concatenate(
+        lax.all_to_all(jnp.stack([own_part] * lax.axis_size(("gz", "gy"))), ("gz", "gy"), 0, 0),
+        axis=1,
+    )
     return (second_image, restricted)
 
 

time: 205 us -> 175 us (0.85)
  waiting for transfers between devices: 116 us -> 81.2 us
  blocking collectives: 0 us -> 20.5 us
  between operations: 14.5 us -> 1.14 us
    all_gather x1 -> x0, waiting for transfers between devices: 34.9 us -> none  [per_device(): restricted = lax.all_gather(own_part, ('gz', 'gy'), axis=1, tiled=True)]
    all_to_all x0 -> x1, blocking collectives: none -> 20.5 us  [per_device(): lax.all_to_all(jnp.stack([own_part] * lax.axis_size(('gz', 'gy'))), ('gz'...]
  transfers between devices with their start and end apart: 16 -> 15, of which waited for: 10 -> 9; matrix products, arithmetic and copies ran while one was open for 3% -> 4% of each run, Pallas kernels for 0% -> 0%
where the time goes in v1:
time: 175 us; the launch traced here: 174 us
  waiting for transfers between devices  81.2 us (46%)
  starting transfers between devices  60.4 us (35%)
  blocking collectives  20.5 us (12%)
  matrix products  6.46 us (4%)
  local copies, waits for them, and re-layouts  3.66 us (2%)
    ppermute x6, waiting for transfers between devices, padded_2(): lax.ppermute(lax.slice_in_dim(block, block.shape[dim] - width, None, axis...  52.6 us
    ppermute x6, starting transfers between devices, padded_2(): lax.ppermute(lax.slice_in_dim(block, 0, width, axis=dim), axis, backward)  32.9 us
    ppermute x6, waiting for transfers between devices, padded_2(): lax.ppermute(lax.slice_in_dim(block, 0, width, axis=dim), axis, backward)  28.6 us
    all_to_all x1, blocking collectives, per_device(): lax.all_to_all(jnp.stack([own_part] * lax.axis_size(('gz', 'gy'))), ('gz'...  20.5 us
    ppermute x6, starting transfers between devices, padded_2(): lax.ppermute(lax.slice_in_dim(block, block.shape[dim] - width, None, axis...  19.9 us
    ppermute x3, starting transfers between devices, shifted(): return lax.ppermute(block, axis, route)  7.56 us
    dot_general x18, matrix products, apply_block(): jnp.einsum('tzyxij,tzyxrj->tzyxri', blocks, vector, preferred_element_typ...  6.17 us
  transfers between devices with their start and end apart: 15, of which 9 were waited for; matrix products, arithmetic and copies ran while one was open for 4% of the time, Pallas kernels for 0%

profile of v1, /device:TPU:1, one launch (start us, length us, event | category | flops | bytes accessed | tf_op | source)
XLA Modules:
  0.0 174.4 jit_solution(12960062086189796495)
XLA Ops:
  0.6 4.5 %collective-permute-start.1 = (bf16[1,2,2,2,256,128]{5,4,3,2,1,0:T(8,128)(2,1)}, bf16[1,2,2,2,256,128]{5,4,3,2,1,0:T(8,128)(2,1)S(1)}, u32[]{:S(2)}, u32[]{:S(2)}) collective-permute-start(bf16[1,2,2,2,256,128]{5,4,3,2,1,0:T(8,128)(2,1)} %param.5), channel_id=1, source_target_pairs={{0,16},{16,32},{32,48},{48,64},{64,80},{80,96},{96,112},{112,128},... | collective-permute-start | bytes 1572872 | tf_op jit(solution)/shard_map/ppermute | solution.py:13
  5.1 12.0 %collective-permute-start = (bf16[1,2,2,2,256,128]{5,4,3,2,1,0:T(8,128)(2,1)}, bf16[1,2,2,2,256,128]{5,4,3,2,1,0:T(8,128)(2,1)S(1)}, u32[]{:S(2)}, u32[]{:S(2)}) collective-permute-start(bf16[1,2,2,2,256,128]{5,4,3,2,1,0:T(8,128)(2,1)} %param.5), channel_id=1, source_target_pairs={{16,0},{32,16},{48,32},{64,48},{80,64},{96,80},{112,96},{128,112},... | collective-permute-start | bytes 1572872 | tf_op jit(solution)/shard_map/ppermute | solution.py:16
  17.1 9.9 %collective-permute-done.1 = bf16[1,2,2,2,256,128]{5,4,3,2,1,0:T(8,128)(2,1)S(1)} collective-permute-done((bf16[1,2,2,2,256,128]{5,4,3,2,1,0:T(8,128)(2,1)}, bf16[1,2,2,2,256,128]{5,4,3,2,1,0:T(8,128)(2,1)S(1)}, u32[]{:S(2)}, u32[]{:S(2)}) %collective-permute-start.1) | collective-permute-done | bytes 524320 | tf_op jit(solution)/shard_map/ppermute | solution.py:13
  27.0 1.1 constant_dynamic-update-slice_fusion.1
  28.4 4.8 %collective-permute-start.2 = (bf16[3,1,2,2,256,128]{5,4,3,2,1,0:T(8,128)(2,1)S(1)}, bf16[3,1,2,2,256,128]{5,4,3,2,1,0:T(8,128)(2,1)S(1)}, u32[]{:S(2)}, u32[]{:S(2)}) collective-permute-start(bf16[3,1,2,2,256,128]{5,4,3,2,1,0:T(8,128)(2,1)S(1)} %get-tuple-element.9), channel_id=1, source_target_pairs={{2,0},{4,2},{6,4},{8,6},{10,8},{12,10},{14,12},{0,14},{3,1},{5,3},... | collective-permute-start | bytes 2359304 | tf_op jit(solution)/shard_map/ppermute | solution.py:16
  33.2 1.9 %collective-permute-start.3 = (bf16[3,1,2,2,256,128]{5,4,3,2,1,0:T(8,128)(2,1)S(1)}, bf16[3,1,2,2,256,128]{5,4,3,2,1,0:T(8,128)(2,1)S(1)}, u32[]{:S(2)}, u32[]{:S(2)}) collective-permute-start(bf16[3,1,2,2,256,128]{5,4,3,2,1,0:T(8,128)(2,1)S(1)} %get-tuple-element.8), channel_id=1, source_target_pairs={{0,2},{2,4},{4,6},{6,8},{8,10},{10,12},{12,14},{14,0},{1,3},{3,5},... | collective-permute-start | bytes 2359304 | tf_op jit(solution)/shard_map/ppermute | solution.py:13
  35.3 3.6 %collective-permute-start.8 = (bf16[1,2,1,2,128,128]{5,4,3,2,1,0:T(8,128)(2,1)S(1)}, bf16[1,2,1,2,128,128]{5,4,3,2,1,0:T(8,128)(2,1)S(1)}, u32[]{:S(2)}, u32[]{:S(2)}) collective-permute-start(bf16[1,2,1,2,128,128]{5,4,3,2,1,0:T(8,128)(2,1)S(1)} %get-tuple-element.23), channel_id=1, source_target_pairs={{1,0},{0,1},{3,2},{2,3},{5,4},{4,5},{7,6},{6,7},{9,8},{8,9},{11,10... | collective-permute-start | bytes 393224 | tf_op jit(solution)/shard_map/ppermute | solution.py:24
  38.9 2.1 %collective-permute-start.6 = (bf16[1,1,2,2,128,128]{5,4,3,2,1,0:T(8,128)(2,1)S(1)}, bf16[1,1,2,2,128,128]{5,4,3,2,1,0:T(8,128)(2,1)S(1)}, u32[]{:S(2)}, u32[]{:S(2)}) collective-permute-start(bf16[1,1,2,2,128,128]{5,4,3,2,1,0:T(8,128)(2,1)S(1)} %get-tuple-element.21), channel_id=1, source_target_pairs={{14,0},{0,2},{2,4},{4,6},{6,8},{8,10},{10,12},{12,14},{15,1},{1,3}... | collective-permute-start | bytes 393224 | tf_op jit(solution)/shard_map/ppermute | solution.py:24
  41.0 1.9 %collective-permute-start.5 = (bf16[1,2,2,2,128,128]{5,4,3,2,1,0:T(8,128)(2,1)S(1)}, bf16[1,2,2,2,128,128]{5,4,3,2,1,0:T(8,128)(2,1)S(1)}, u32[]{:S(2)}, u32[]{:S(2)}) collective-permute-start(bf16[1,2,2,2,128,128]{5,4,3,2,1,0:T(8,128)(2,1)S(1)} %get-tuple-element.10), channel_id=1, source_target_pairs={{496,0},{0,16},{16,32},{32,48},{48,64},{64,80},{80,96},{96,112},{1... | collective-permute-start | bytes 786440 | tf_op jit(solution)/shard_map/ppermute | solution.py:24
  43.2 11.2 %collective-permute-done.2 = bf16[3,1,2,2,256,128]{5,4,3,2,1,0:T(8,128)(2,1)S(1)} collective-permute-done((bf16[3,1,2,2,256,128]{5,4,3,2,1,0:T(8,128)(2,1)S(1)}, bf16[3,1,2,2,256,128]{5,4,3,2,1,0:T(8,128)(2,1)S(1)}, u32[]{:S(2)}, u32[]{:S(2)}) %collective-permute-start.2) | collective-permute-done | bytes 786464 | tf_op jit(solution)/shard_map/ppermute | solution.py:16
  54.4 18.7 %collective-permute-done.3 = bf16[3,1,2,2,256,128]{5,4,3,2,1,0:T(8,128)(2,1)S(1)} collective-permute-done((bf16[3,1,2,2,256,128]{5,4,3,2,1,0:T(8,128)(2,1)S(1)}, bf16[3,1,2,2,256,128]{5,4,3,2,1,0:T(8,128)(2,1)S(1)}, u32[]{:S(2)}, u32[]{:S(2)}) %collective-permute-start.3) | collective-permute-done | bytes 786464 | tf_op jit(solution)/shard_map/ppermute | solution.py:13
  73.1 0.4 pad_maximum_fusion
  73.7 5.5 %collective-permute-start.7 = (bf16[3,4,1,2,256,128]{5,4,3,2,1,0:T(8,128)(2,1)S(1)}, bf16[3,4,1,2,256,128]{5,4,3,2,1,0:T(8,128)(2,1)S(1)}, u32[]{:S(2)}, u32[]{:S(2)}) collective-permute-start(bf16[3,4,1,2,256,128]{5,4,3,2,1,0:T(8,128)(2,1)S(1)} %get-tuple-element.4), channel_id=1, source_target_pairs={{0,1},{1,0},{2,3},{3,2},{4,5},{5,4},{6,7},{7,6},{8,9},{9,8},{10,11... | collective-permute-start | bytes 4718600 | tf_op jit(solution)/shard_map/ppermute | solution.py:13
  79.3 2.1 %collective-permute-start.4 = (bf16[3,4,1,2,256,128]{5,4,3,2,1,0:T(8,128)(2,1)S(1)}, bf16[3,4,1,2,256,128]{5,4,3,2,1,0:T(8,128)(2,1)S(1)}, u32[]{:S(2)}, u32[]{:S(2)}) collective-permute-start(bf16[3,4,1,2,256,128]{5,4,3,2,1,0:T(8,128)(2,1)S(1)} %get-tuple-element.5), channel_id=1, source_target_pairs={{1,0},{0,1},{3,2},{2,3},{5,4},{4,5},{7,6},{6,7},{9,8},{8,9},{11,10... | collective-permute-start | bytes 4718600 | tf_op jit(solution)/shard_map/ppermute | solution.py:16
  83.4 1.3 collective-permute-done.4
  85.0 0.6 fusion.15
  85.7 1.9 %collective-permute-start.10 = (bf16[1,2,2,2,256,128]{5,4,3,2,1,0:T(8,128)(2,1)S(1)}, bf16[1,2,2,2,256,128]{5,4,3,2,1,0:T(8,128)(2,1)S(1)}, u32[]{:S(2)}, u32[]{:S(2)}) collective-permute-start(bf16[1,2,2,2,256,128]{5,4,3,2,1,0:T(8,128)(2,1)S(1)} %fusion.15), channel_id=1, source_target_pairs={{0,16},{16,32},{32,48},{48,64},{64,80},{80,96},{96,112},{112,128},... | collective-permute-start | bytes 1572872 | tf_op jit(solution)/shard_map/ppermute | solution.py:13
  87.6 7.0 %collective-permute-start.9 = (bf16[1,2,2,2,256,128]{5,4,3,2,1,0:T(8,128)(2,1)S(1)}, bf16[1,2,2,2,256,128]{5,4,3,2,1,0:T(8,128)(2,1)S(1)}, u32[]{:S(2)}, u32[]{:S(2)}) collective-permute-start(bf16[1,2,2,2,256,128]{5,4,3,2,1,0:T(8,128)(2,1)S(1)} %fusion.15), channel_id=1, source_target_pairs={{16,0},{32,16},{48,32},{64,48},{80,64},{96,80},{112,96},{128,112},... | collective-permute-start | bytes 1572872 | tf_op jit(solution)/shard_map/ppermute | solution.py:16
  94.6 9.9 %collective-permute-done.10 = bf16[1,2,2,2,256,128]{5,4,3,2,1,0:T(8,128)(2,1)S(1)} collective-permute-done((bf16[1,2,2,2,256,128]{5,4,3,2,1,0:T(8,128)(2,1)S(1)}, bf16[1,2,2,2,256,128]{5,4,3,2,1,0:T(8,128)(2,1)S(1)}, u32[]{:S(2)}, u32[]{:S(2)}) %collective-permute-start.10) | collective-permute-done | bytes 524320 | tf_op jit(solution)/shard_map/ppermute | solution.py:13
  104.5 0.9 collective-permute-done.9
  105.7 2.2 %collective-permute-start.12 = (bf16[3,1,2,2,256,128]{5,4,3,2,1,0:T(8,128)(2,1)S(1)}, bf16[3,1,2,2,256,128]{5,4,3,2,1,0:T(8,128)(2,1)S(1)}, u32[]{:S(2)}, u32[]{:S(2)}) collective-permute-start(bf16[3,1,2,2,256,128]{5,4,3,2,1,0:T(8,128)(2,1)S(1)} %get-tuple-element.6), channel_id=1, source_target_pairs={{0,2},{2,4},{4,6},{6,8},{8,10},{10,12},{12,14},{14,0},{1,3},{3,5},... | collective-permute-start | bytes 2359304 | tf_op jit(solution)/shard_map/ppermute | solution.py:13
  107.9 5.2 %collective-permute-start.11 = (bf16[3,1,2,2,256,128]{5,4,3,2,1,0:T(8,128)(2,1)S(1)}, bf16[3,1,2,2,256,128]{5,4,3,2,1,0:T(8,128)(2,1)S(1)}, u32[]{:S(2)}, u32[]{:S(2)}) collective-permute-start(bf16[3,1,2,2,256,128]{5,4,3,2,1,0:T(8,128)(2,1)S(1)} %get-tuple-element.7), channel_id=1, source_target_pairs={{2,0},{4,2},{6,4},{8,6},{10,8},{12,10},{14,12},{0,14},{3,1},{5,3},... | collective-permute-start | bytes 2359304 | tf_op jit(solution)/shard_map/ppermute | solution.py:16
  113.4 14.1 %collective-permute-done.12 = bf16[3,1,2,2,256,128]{5,4,3,2,1,0:T(8,128)(2,1)S(1)} collective-permute-done((bf16[3,1,2,2,256,128]{5,4,3,2,1,0:T(8,128)(2,1)S(1)}, bf16[3,1,2,2,256,128]{5,4,3,2,1,0:T(8,128)(2,1)S(1)}, u32[]{:S(2)}, u32[]{:S(2)}) %collective-permute-start.12) | collective-permute-done | bytes 786464 | tf_op jit(solution)/shard_map/ppermute | solution.py:13
  127.5 13.9 %collective-permute-done.11 = bf16[3,1,2,2,256,128]{5,4,3,2,1,0:T(8,128)(2,1)S(1)} collective-permute-done((bf16[3,1,2,2,256,128]{5,4,3,2,1,0:T(8,128)(2,1)S(1)}, bf16[3,1,2,2,256,128]{5,4,3,2,1,0:T(8,128)(2,1)S(1)}, u32[]{:S(2)}, u32[]{:S(2)}) %collective-permute-start.11) | collective-permute-done | bytes 786464 | tf_op jit(solution)/shard_map/ppermute | solution.py:16
  141.4 0.4 pad_maximum_fusion.1
  142.0 3.8 %collective-permute-start.14 = (bf16[3,4,1,2,256,128]{5,4,3,2,1,0:T(8,128)(2,1)S(1)}, bf16[3,4,1,2,256,128]{5,4,3,2,1,0:T(8,128)(2,1)S(1)}, u32[]{:S(2)}, u32[]{:S(2)}) collective-permute-start(bf16[3,4,1,2,256,128]{5,4,3,2,1,0:T(8,128)(2,1)S(1)} %get-tuple-element.2), channel_id=1, source_target_pairs={{0,1},{1,0},{2,3},{3,2},{4,5},{5,4},{6,7},{7,6},{8,9},{9,8},{10,11... | collective-permute-start | bytes 4718600 | tf_op jit(solution)/shard_map/ppermute | solution.py:13
  145.8 1.9 %collective-permute-start.13 = (bf16[3,4,1,2,256,128]{5,4,3,2,1,0:T(8,128)(2,1)S(1)}, bf16[3,4,1,2,256,128]{5,4,3,2,1,0:T(8,128)(2,1)S(1)}, u32[]{:S(2)}, u32[]{:S(2)}) collective-permute-start(bf16[3,4,1,2,256,128]{5,4,3,2,1,0:T(8,128)(2,1)S(1)} %get-tuple-element.3), channel_id=1, source_target_pairs={{1,0},{0,1},{3,2},{2,3},{5,4},{4,5},{7,6},{6,7},{9,8},{8,9},{11,10... | collective-permute-start | bytes 4718600 | tf_op jit(solution)/shard_map/ppermute | solution.py:16
  149.8 1.4 collective-permute-done.13
  151.2 0.3 fusion.32
  151.5 0.7 fusion.14
  152.9 20.5 %all_to_all.5 = bf16[16,1,1,256,128]{4,3,2,1,0:T(8,128)(2,1)S(1)} all-to-all(bf16[16,1,1,256,128]{4,3,2,1,0:T(8,128)(2,1)S(1)} %stack.3), channel_id=1, replica_groups=mesh['ta'=32,'gz'=8,'gy'=2] {'gz','gy'}, dimensions={0} | all-to-all | bytes 2097152 | tf_op jit(solution)/shard_map/all_to_all | solution.py:75
  173.5 1.0 copy.19
  (51 shorter events, 6.7 us)
Async XLA Ops:
  0.6 81.2 %copy-start = (bf16[1,2,2,2,128,128]{5,4,3,2,1,0:T(8,128)(2,1)S(1)}, bf16[1,2,2,2,128,128]{5,4,3,2,1,0:T(8,128)(2,1)}, u32[]{:S(2)}) copy-start(bf16[1,2,2,2,128,128]{5,4,3,2,1,0:T(8,128)(2,1)} %param.6) | copy-start | bytes 786436
  0.6 26.4 %collective-permute-start.1 = (bf16[1,2,2,2,256,128]{5,4,3,2,1,0:T(8,128)(2,1)}, bf16[1,2,2,2,256,128]{5,4,3,2,1,0:T(8,128)(2,1)S(1)}, u32[]{:S(2)}, u32[]{:S(2)}) collective-permute-start(bf16[1,2,2,2,256,128]{5,4,3,2,1,0:T(8,128)(2,1)} %param.5), channel_id=1, source_target_pairs={{0,16},{16,32},{32,48},{48,64},{64,80},{80,96},{96,112},{112,128},... | collective-permute-start | bytes 1572872 | tf_op jit(solution)/shard_map/ppermute | solution.py:13
  5.1 23.0 %collective-permute-start = (bf16[1,2,2,2,256,128]{5,4,3,2,1,0:T(8,128)(2,1)}, bf16[1,2,2,2,256,128]{5,4,3,2,1,0:T(8,128)(2,1)S(1)}, u32[]{:S(2)}, u32[]{:S(2)}) collective-permute-start(bf16[1,2,2,2,256,128]{5,4,3,2,1,0:T(8,128)(2,1)} %param.5), channel_id=1, source_target_pairs={{16,0},{32,16},{48,32},{64,48},{80,64},{96,80},{112,96},{128,112},... | collective-permute-start | bytes 1572872 | tf_op jit(solution)/shard_map/ppermute | solution.py:16
  28.3 6.9 %copy-start.3 = (bf16[4,1,2,2,2,128,128]{6,5,4,3,2,1,0:T(8,128)(2,1)S(1)}, bf16[4,1,2,2,2,128,128]{6,5,4,3,2,1,0:T(8,128)(2,1)}, u32[]{:S(2)}) copy-start(bf16[4,1,2,2,2,128,128]{6,5,4,3,2,1,0:T(8,128)(2,1)} %param.8) | copy-start | bytes 3145732
  28.4 14.5 %copy-start.1 = (bf16[1,2,2,2,256,128]{5,4,3,2,1,0:T(8,128)(2,1)S(1)}, bf16[1,2,2,2,256,128]{5,4,3,2,1,0:T(8,128)(2,1)}, u32[]{:S(2)}) copy-start(bf16[1,2,2,2,256,128]{5,4,3,2,1,0:T(8,128)(2,1)} %param.5) | copy-start | bytes 1572868
  28.4 25.9 %collective-permute-start.2 = (bf16[3,1,2,2,256,128]{5,4,3,2,1,0:T(8,128)(2,1)S(1)}, bf16[3,1,2,2,256,128]{5,4,3,2,1,0:T(8,128)(2,1)S(1)}, u32[]{:S(2)}, u32[]{:S(2)}) collective-permute-start(bf16[3,1,2,2,256,128]{5,4,3,2,1,0:T(8,128)(2,1)S(1)} %get-tuple-element.9), channel_id=1, source_target_pairs={{2,0},{4,2},{6,4},{8,6},{10,8},{12,10},{14,12},{0,14},{3,1},{5,3},... | collective-permute-start | bytes 2359304 | tf_op jit(solution)/shard_map/ppermute | solution.py:16
  33.2 39.9 %collective-permute-start.3 = (bf16[3,1,2,2,256,128]{5,4,3,2,1,0:T(8,128)(2,1)S(1)}, bf16[3,1,2,2,256,128]{5,4,3,2,1,0:T(8,128)(2,1)S(1)}, u32[]{:S(2)}, u32[]{:S(2)}) collective-permute-start(bf16[3,1,2,2,256,128]{5,4,3,2,1,0:T(8,128)(2,1)S(1)} %get-tuple-element.8), channel_id=1, source_target_pairs={{0,2},{2,4},{4,6},{6,8},{8,10},{10,12},{12,14},{14,0},{1,3},{3,5},... | collective-permute-start | bytes 2359304 | tf_op jit(solution)/shard_map/ppermute | solution.py:13
  35.3 47.8 %collective-permute-start.8 = (bf16[1,2,1,2,128,128]{5,4,3,2,1,0:T(8,128)(2,1)S(1)}, bf16[1,2,1,2,128,128]{5,4,3,2,1,0:T(8,128)(2,1)S(1)}, u32[]{:S(2)}, u32[]{:S(2)}) collective-permute-start(bf16[1,2,1,2,128,128]{5,4,3,2,1,0:T(8,128)(2,1)S(1)} %get-tuple-element.23), channel_id=1, source_target_pairs={{1,0},{0,1},{3,2},{2,3},{5,4},{4,5},{7,6},{6,7},{9,8},{8,9},{11,10... | collective-permute-start | bytes 393224 | tf_op jit(solution)/shard_map/ppermute | solution.py:24
  38.9 43.9 %collective-permute-start.6 = (bf16[1,1,2,2,128,128]{5,4,3,2,1,0:T(8,128)(2,1)S(1)}, bf16[1,1,2,2,128,128]{5,4,3,2,1,0:T(8,128)(2,1)S(1)}, u32[]{:S(2)}, u32[]{:S(2)}) collective-permute-start(bf16[1,1,2,2,128,128]{5,4,3,2,1,0:T(8,128)(2,1)S(1)} %get-tuple-element.21), channel_id=1, source_target_pairs={{14,0},{0,2},{2,4},{4,6},{6,8},{8,10},{10,12},{12,14},{15,1},{1,3}... | collective-permute-start | bytes 393224 | tf_op jit(solution)/shard_map/ppermute | solution.py:24
  41.0 41.5 %collective-permute-start.5 = (bf16[1,2,2,2,128,128]{5,4,3,2,1,0:T(8,128)(2,1)S(1)}, bf16[1,2,2,2,128,128]{5,4,3,2,1,0:T(8,128)(2,1)S(1)}, u32[]{:S(2)}, u32[]{:S(2)}) collective-permute-start(bf16[1,2,2,2,128,128]{5,4,3,2,1,0:T(8,128)(2,1)S(1)} %get-tuple-element.10), channel_id=1, source_target_pairs={{496,0},{0,16},{16,32},{32,48},{48,64},{64,80},{80,96},{96,112},{1... | collective-permute-start | bytes 786440 | tf_op jit(solution)/shard_map/ppermute | solution.py:24
  73.7 9.3 %collective-permute-start.7 = (bf16[3,4,1,2,256,128]{5,4,3,2,1,0:T(8,128)(2,1)S(1)}, bf16[3,4,1,2,256,128]{5,4,3,2,1,0:T(8,128)(2,1)S(1)}, u32[]{:S(2)}, u32[]{:S(2)}) collective-permute-start(bf16[3,4,1,2,256,128]{5,4,3,2,1,0:T(8,128)(2,1)S(1)} %get-tuple-element.4), channel_id=1, source_target_pairs={{0,1},{1,0},{2,3},{3,2},{4,5},{5,4},{6,7},{7,6},{8,9},{9,8},{10,11... | collective-permute-start | bytes 4718600 | tf_op jit(solution)/shard_map/ppermute | solution.py:13
  79.3 2.2 %copy-start.2 = (bf16[4,1,2,2,2,128,128]{6,5,4,3,2,1,0:T(8,128)(2,1)S(1)}, bf16[4,1,2,2,2,128,128]{6,5,4,3,2,1,0:T(8,128)(2,1)}, u32[]{:S(2)}) copy-start(bf16[4,1,2,2,2,128,128]{6,5,4,3,2,1,0:T(8,128)(2,1)} %param.7) | copy-start | bytes 3145732
  79.3 5.4 %collective-permute-start.4 = (bf16[3,4,1,2,256,128]{5,4,3,2,1,0:T(8,128)(2,1)S(1)}, bf16[3,4,1,2,256,128]{5,4,3,2,1,0:T(8,128)(2,1)S(1)}, u32[]{:S(2)}, u32[]{:S(2)}) collective-permute-start(bf16[3,4,1,2,256,128]{5,4,3,2,1,0:T(8,128)(2,1)S(1)} %get-tuple-element.5), channel_id=1, source_target_pairs={{1,0},{0,1},{3,2},{2,3},{5,4},{4,5},{7,6},{6,7},{9,8},{8,9},{11,10... | collective-permute-start | bytes 4718600 | tf_op jit(solution)/shard_map/ppermute | solution.py:16
  85.7 18.8 %collective-permute-start.10 = (bf16[1,2,2,2,256,128]{5,4,3,2,1,0:T(8,128)(2,1)S(1)}, bf16[1,2,2,2,256,128]{5,4,3,2,1,0:T(8,128)(2,1)S(1)}, u32[]{:S(2)}, u32[]{:S(2)}) collective-permute-start(bf16[1,2,2,2,256,128]{5,4,3,2,1,0:T(8,128)(2,1)S(1)} %fusion.15), channel_id=1, source_target_pairs={{0,16},{16,32},{32,48},{48,64},{64,80},{80,96},{96,112},{112,128},... | collective-permute-start | bytes 1572872 | tf_op jit(solution)/shard_map/ppermute | solution.py:13
  87.6 17.8 %collective-permute-start.9 = (bf16[1,2,2,2,256,128]{5,4,3,2,1,0:T(8,128)(2,1)S(1)}, bf16[1,2,2,2,256,128]{5,4,3,2,1,0:T(8,128)(2,1)S(1)}, u32[]{:S(2)}, u32[]{:S(2)}) collective-permute-start(bf16[1,2,2,2,256,128]{5,4,3,2,1,0:T(8,128)(2,1)S(1)} %fusion.15), channel_id=1, source_target_pairs={{16,0},{32,16},{48,32},{64,48},{80,64},{96,80},{112,96},{128,112},... | collective-permute-start | bytes 1572872 | tf_op jit(solution)/shard_map/ppermute | solution.py:16
  105.7 21.8 %collective-permute-start.12 = (bf16[3,1,2,2,256,128]{5,4,3,2,1,0:T(8,128)(2,1)S(1)}, bf16[3,1,2,2,256,128]{5,4,3,2,1,0:T(8,128)(2,1)S(1)}, u32[]{:S(2)}, u32[]{:S(2)}) collective-permute-start(bf16[3,1,2,2,256,128]{5,4,3,2,1,0:T(8,128)(2,1)S(1)} %get-tuple-element.6), channel_id=1, source_target_pairs={{0,2},{2,4},{4,6},{6,8},{8,10},{10,12},{12,14},{14,0},{1,3},{3,5},... | collective-permute-start | bytes 2359304 | tf_op jit(solution)/shard_map/ppermute | solution.py:13
  107.9 33.4 %collective-permute-start.11 = (bf16[3,1,2,2,256,128]{5,4,3,2,1,0:T(8,128)(2,1)S(1)}, bf16[3,1,2,2,256,128]{5,4,3,2,1,0:T(8,128)(2,1)S(1)}, u32[]{:S(2)}, u32[]{:S(2)}) collective-permute-start(bf16[3,1,2,2,256,128]{5,4,3,2,1,0:T(8,128)(2,1)S(1)} %get-tuple-element.7), channel_id=1, source_target_pairs={{2,0},{4,2},{6,4},{8,6},{10,8},{12,10},{14,12},{0,14},{3,1},{5,3},... | collective-permute-start | bytes 2359304 | tf_op jit(solution)/shard_map/ppermute | solution.py:16
  142.0 7.4 %collective-permute-start.14 = (bf16[3,4,1,2,256,128]{5,4,3,2,1,0:T(8,128)(2,1)S(1)}, bf16[3,4,1,2,256,128]{5,4,3,2,1,0:T(8,128)(2,1)S(1)}, u32[]{:S(2)}, u32[]{:S(2)}) collective-permute-start(bf16[3,4,1,2,256,128]{5,4,3,2,1,0:T(8,128)(2,1)S(1)} %get-tuple-element.2), channel_id=1, source_target_pairs={{0,1},{1,0},{2,3},{3,2},{4,5},{5,4},{6,7},{7,6},{8,9},{9,8},{10,11... | collective-permute-start | bytes 4718600 | tf_op jit(solution)/shard_map/ppermute | solution.py:13
  145.8 5.3 %collective-permute-start.13 = (bf16[3,4,1,2,256,128]{5,4,3,2,1,0:T(8,128)(2,1)S(1)}, bf16[3,4,1,2,256,128]{5,4,3,2,1,0:T(8,128)(2,1)S(1)}, u32[]{:S(2)}, u32[]{:S(2)}) collective-permute-start(bf16[3,4,1,2,256,128]{5,4,3,2,1,0:T(8,128)(2,1)S(1)} %get-tuple-element.3), channel_id=1, source_target_pairs={{1,0},{0,1},{3,2},{2,3},{5,4},{4,5},{7,6},{6,7},{9,8},{8,9},{11,10... | collective-permute-start | bytes 4718600 | tf_op jit(solution)/shard_map/ppermute | solution.py:16
  151.5 1.0 copy-start.5
  152.4 21.0 %copy-start.4 = (bf16[1,2,2,2,256,128]{5,4,3,2,1,0:T(8,128)(2,1)}, bf16[1,2,2,2,256,128]{5,4,3,2,1,0:T(8,128)(2,1)S(1)}, u32[]{:S(2)}) copy-start(bf16[1,2,2,2,256,128]{5,4,3,2,1,0:T(8,128)(2,1)S(1)} %fusion.14) | copy-start | bytes 1572868
